TPU v7x, 32 devices: a whole 2x2x4 slice. The times are simulated.
32 devices in a mesh: rows: 8 (over z, x), cols: 4 (over y, core).
Axes of the slice: x: 2, y: 2, z: 4, core: 2. Of those that a mesh axis runs over, the one named last changes fastest.
Arguments:
- vectors: bfloat16 [64, 131072], P('cols', 'rows'), may hold values from -110 to 110
- tile_vals: bfloat16 [1536, 256, 256], P('rows'), may hold values from -0.21875 to 0.21875
- tile_row: int32 [8, 192], P('rows'), may hold values from 0 to 63
- tile_src: int32 [8, 192], P('rows'), may hold values from 0 to 191, each once within a row
- send_list: int32 [64, 16], P('rows'), may hold values from 0 to 63
- ritz_matrix: bfloat16 [64, 64], P(None, 'cols'), may hold values from -0.75 to 0.75
Outputs:
- rotated: bfloat16 [64, 131072], P('cols', 'rows')
- gram_matrix: float32 [64, 64], P('cols')
- projected: float32 [64, 64], P('cols')
Inputs may be any that keep to these rules, and one draw needn't show every extreme that they name: Each row of tile_src holds every number once, so that each own or received block is read by exactly one tile.
All inputs are finite; a program needn't handle non-finite values.
Results may differ from a plain program's by a relative error of at most 0.0062.
Values may be sent and summed in bfloat16 or wider, within the bound.
No kernel may reach another device: no remote copies, remote signals or barrier semaphores. Data moves between devices by JAX's collectives and lax.ppermute only.
A program may use at most 128 MiB of HBM per device.

v0:
```python
import jax
import jax.numpy as jnp
from jax import lax
from jax.sharding import PartitionSpec as P


def tile_products(sources, tile_block, row_ids, src_ids, nblocks):
    chosen = jnp.take(sources, src_ids, axis=1)
    products = jnp.einsum("ktc,trc->ktr", chosen, tile_block, preferred_element_type=jnp.float32)
    onehot = (row_ids[None, :] == jnp.arange(nblocks, dtype=jnp.int32)[:, None]).astype(jnp.float32)
    summed = jnp.einsum("bt,ktr->kbr", onehot, products, precision=lax.Precision.HIGHEST)
    return summed.reshape(summed.shape[0], -1)


def apply_operator(vectors, tile_vals, tile_row, tile_src, send_list):
    columns, length = vectors.shape
    tile_side = tile_vals.shape[1]
    nblocks = length // tile_side
    blocked = vectors.reshape(columns, nblocks, tile_side)
    outgoing = jnp.take(blocked, send_list.reshape(-1), axis=1)
    incoming = lax.all_to_all(outgoing, "rows", split_axis=1, concat_axis=1, tiled=True)
    row_ids = tile_row.reshape(-1)
    src_ids = tile_src.reshape(-1)
    sources = jnp.concatenate([blocked, incoming], axis=1)
    return tile_products(sources, tile_vals, row_ids, src_ids, nblocks)


def contract_nodes(left_side, right_side):
    return lax.dot_general(
        left_side, right_side, (((1,), (1,)), ((), ())), preferred_element_type=jnp.float32
    )


def body(vectors, tile_vals, tile_row, tile_src, send_list, ritz_matrix):
    first_pass = apply_operator(vectors, tile_vals, tile_row, tile_src, send_list).astype(
        jnp.bfloat16
    )
    second = apply_operator(first_pass, tile_vals, tile_row, tile_src, send_list)
    filtered = (2.0 * second - vectors.astype(jnp.float32)).astype(jnp.bfloat16)
    total_nodes = vectors.shape[1] * lax.axis_size("rows")
    operated = apply_operator(filtered, tile_vals, tile_row, tile_src, send_list).astype(
        jnp.bfloat16
    )
    portion = lax.all_gather(filtered, "cols", axis=0, tiled=True)
    gram_piece = contract_nodes(filtered, portion)
    proj_piece = contract_nodes(operated, portion)
    turned = lax.dot_general(
        ritz_matrix, portion, (((0,), (0,)), ((), ())), preferred_element_type=jnp.float32
    )
    gram_total, proj_total = lax.psum((gram_piece, proj_piece), "rows")
    gram_matrix = gram_total / total_nodes
    projected = proj_total / total_nodes
    rotated = turned.astype(jnp.bfloat16)
    return (rotated, gram_matrix, projected)


def solution(mesh):
    return jax.shard_map(
        body,
        mesh=mesh,
        in_specs=(
            P("cols", "rows"),
            P("rows", None, None),
            P("rows", None),
            P("rows", None),
            P("rows", None),
            P(None, "cols"),
        ),
        out_specs=(P("cols", "rows"), P("cols", None), P("cols", None)),
        check_vma=False,
    )
```

profile of v0, /device:TPU:0, one launch (start us, length us, event | category | flops | bytes accessed | tf_op | source)
XLA Modules:
  0.0 207.6 jit_solution(13215640300237485455)
XLA Ops:
  7.2 0.8 reshape.40
  8.0 1.1 copy.41
  9.7 1.2 select_bitcast_fusion.2
  10.9 7.4 %all-to-all-start = ((bf16[16,128,256]{2,0,1:T(8,128)(2,1)}), bf16[16,128,256]{2,0,1:T(8,128)(2,1)S(1)}, u32[]{:S(2)}, u32[]{:S(2)}) async-start(bf16[16,128,256]{2,0,1:T(8,128)(2,1)} %select_bitcast_fusion.2), calls=%async_computation | async-start | bytes 2097152 | tf_op jit(solution)/shard_map/all_to_all | solution.py:21
  18.4 25.7 %all-to-all-done = bf16[16,128,256]{2,0,1:T(8,128)(2,1)S(1)} async-done(((bf16[16,128,256]{2,0,1:T(8,128)(2,1)}), bf16[16,128,256]{2,0,1:T(8,128)(2,1)S(1)}, u32[]{:S(2)}, u32[]{:S(2)}) %all-to-all-start) | async-done | bytes 1048608 | tf_op jit(solution)/shard_map/all_to_all | solution.py:21
  44.2 2.0 gather_fusion.1
  46.3 12.0 %convolution_bitcast_fusion.2 = f32[16,192,256]{2,0,1:T(8,128)S(1)} fusion(bf16[192,256,256]{2,1,0:T(8,128)(2,1)} %param.11, bf16[192,16,256]{2,1,0:T(8,128)(2,1)} %gather_fusion.1, pred[192]{0:T(512)(128)(4,1)S(1)} %compare_and_fusion), kind=kOutput, calls=%fused_computation.16 | convolution fusion | flops 403439616 | bytes 29884608 | tf_op jit(solution)/shard_map/ktc,trc->ktr/dot_general | solution.py:9
  58.3 3.2 %fusion.25 = bf16[16,64,256]{2,1,0:T(8,128)(2,1)S(1)} fusion(f32[16,192,256]{2,0,1:T(8,128)S(1)} %convolution_bitcast_fusion.2, s32[192]{0:T(256)S(1)} %bitcast.65), kind=kOutput, calls=%fused_computation.32 | convolution fusion | flops 604254208 | bytes 3670784 | tf_op jit(solution)/shard_map/bt,ktr->kbr/dot_general | solution.py:11
  62.6 29.3 %all_to_all.15 = bf16[16,128,256]{2,0,1:T(8,128)(2,1)S(1)} all-to-all(bf16[16,128,256]{2,0,1:T(8,128)(2,1)S(1)} %select_bitcast_fusion.1), channel_id=1, replica_groups=mesh['rows'=8,'cols'=4] {'rows'}, dimensions={1} | all-to-all | bytes 2097152 | tf_op jit(solution)/shard_map/all_to_all | solution.py:21
  92.1 2.0 gather_fusion.3
  94.1 12.0 %convolution_bitcast_fusion.1 = f32[16,192,256]{2,0,1:T(8,128)S(1)} fusion(bf16[192,256,256]{2,1,0:T(8,128)(2,1)} %param.11, bf16[192,16,256]{2,1,0:T(8,128)(2,1)} %gather_fusion.3, pred[192]{0:T(512)(128)(4,1)S(1)} %compare_and_fusion), kind=kOutput, calls=%fused_computation.15 | convolution fusion | flops 403439616 | bytes 29884608 | tf_op jit(solution)/shard_map/ktc,trc->ktr/dot_general | solution.py:9
  106.1 3.2 %fusion.16 = f32[16,256,64]{1,2,0:T(8,128)S(1)} fusion(f32[16,192,256]{2,0,1:T(8,128)S(1)} %convolution_bitcast_fusion.1, s32[192]{0:T(256)S(1)} %bitcast.66), kind=kOutput, calls=%fused_computation.29 | convolution fusion | flops 604254208 | bytes 4195072 | tf_op jit(solution)/shard_map/bt,ktr->kbr/dot_general | solution.py:11
  110.5 0.6 gather_fusion.4
  111.2 1.2 select_bitcast_fusion
  112.4 4.2 %all-to-all-start.2 = ((bf16[16,128,256]{2,0,1:T(8,128)(2,1)}), bf16[16,128,256]{2,0,1:T(8,128)(2,1)}, u32[]{:S(2)}, u32[]{:S(2)}) async-start(bf16[16,128,256]{2,0,1:T(8,128)(2,1)} %select_bitcast_fusion), calls=%async_computation.2 | async-start | bytes 2097152 | tf_op jit(solution)/shard_map/all_to_all | solution.py:21
  117.4 24.4 %all-to-all-done.2 = bf16[16,128,256]{2,0,1:T(8,128)(2,1)} async-done(((bf16[16,128,256]{2,0,1:T(8,128)(2,1)}), bf16[16,128,256]{2,0,1:T(8,128)(2,1)}, u32[]{:S(2)}, u32[]{:S(2)}) %all-to-all-start.2) | async-done | bytes 1048608 | tf_op jit(solution)/shard_map/all_to_all | solution.py:21
  141.8 1.4 pad_maximum_fusion.2
  143.2 2.0 gather_fusion.5
  145.2 12.0 %convolution_bitcast_fusion = f32[16,192,256]{2,0,1:T(8,128)S(1)} fusion(bf16[192,256,256]{2,1,0:T(8,128)(2,1)} %param.11, bf16[192,16,256]{2,1,0:T(8,128)(2,1)} %gather_fusion.5, pred[192]{0:T(512)(128)(4,1)S(1)} %compare_and_fusion), kind=kOutput, calls=%fused_computation.14 | convolution fusion | flops 403439616 | bytes 29884608 | tf_op jit(solution)/shard_map/ktc,trc->ktr/dot_general | solution.py:9
  157.2 3.2 %fusion.22 = bf16[16,256,64]{1,2,0:T(8,128)(2,1)S(1)} fusion(f32[16,192,256]{2,0,1:T(8,128)S(1)} %convolution_bitcast_fusion, s32[192]{0:T(256)S(1)} %bitcast.67), kind=kOutput, calls=%fused_computation.31 | convolution fusion | flops 604254208 | bytes 3670784 | tf_op jit(solution)/shard_map/bt,ktr->kbr/dot_general | solution.py:11
  160.7 2.5 %fusion.41 = f32[16,64]{1,0:T(8,128)S(1)} fusion(bf16[16,16384]{1,0:T(8,128)(2,1)} %copy-done.2, bf16[64,16384]{1,0:T(8,128)(2,1)} %all-gather.2.cloned.1.call-done), kind=kOutput, calls=%fused_computation.58 | convolution fusion | flops 33554432 | bytes 2625536 | tf_op jit(solution)/shard_map/dot_general | solution.py:29
  163.3 0.7 fusion.42
  163.9 35.0 %all-reduce = (f32[16,64]{1,0:T(8,128)S(1)}, f32[16,64]{1,0:T(8,128)S(1)}) all-reduce(f32[16,64]{1,0:T(8,128)S(1)} %fusion.41, f32[16,64]{1,0:T(8,128)S(1)} %fusion.42), channel_id=1, replica_groups=mesh['rows'=8,'cols'=4] {'rows'}, use_global_device_ids=true, to_apply=%region_0.3 | all-reduce | flops 2048 | bytes 16384 | tf_op jit(solution)/shard_map/psum | solution.py:50
  199.5 1.2 fusion
  (32 shorter events, 5.0 us)
Async XLA Ops:
  7.2 192.4 %copy-start = (bf16[64,16]{0,1:T(8,128)(2,1)S(1)}, bf16[64,16]{0,1:T(8,128)(2,1)}, u32[]{:S(2)}) copy-start(bf16[64,16]{0,1:T(8,128)(2,1)} %param.15) | copy-start | bytes 6148
  10.9 7.4 %copy-start.5 = (s32[1,192]{1,0:T(1,128)S(1)}, s32[1,192]{1,0:T(1,128)}, u32[]{:S(2)}) copy-start(s32[1,192]{1,0:T(1,128)} %param.13) | copy-start | bytes 2308
  10.9 33.2 %all-to-all-start = ((bf16[16,128,256]{2,0,1:T(8,128)(2,1)}), bf16[16,128,256]{2,0,1:T(8,128)(2,1)S(1)}, u32[]{:S(2)}, u32[]{:S(2)}) async-start(bf16[16,128,256]{2,0,1:T(8,128)(2,1)} %select_bitcast_fusion.2), calls=%async_computation | async-start | bytes 2097152 | tf_op jit(solution)/shard_map/all_to_all | solution.py:21
  46.3 12.1 %copy-start.4 = (s32[1,192]{1,0:T(1,128)S(1)}, s32[1,192]{1,0:T(1,128)}, u32[]{:S(2)}) copy-start(s32[1,192]{1,0:T(1,128)} %param.12) | copy-start | bytes 2308
  109.3 1.0 copy-start.3
  110.4 0.8 copy-start.2
  112.4 29.4 %all-to-all-start.2 = ((bf16[16,128,256]{2,0,1:T(8,128)(2,1)}), bf16[16,128,256]{2,0,1:T(8,128)(2,1)}, u32[]{:S(2)}, u32[]{:S(2)}) async-start(bf16[16,128,256]{2,0,1:T(8,128)(2,1)} %select_bitcast_fusion), calls=%async_computation.2 | async-start | bytes 2097152 | tf_op jit(solution)/shard_map/all_to_all | solution.py:21
  116.7 44.0 %all-gather.2.cloned.1.call-start = ((), (), s32[]{:S(2)}) async-start(), calls=%async_computation.3 | async-start | bytes 2621440 | tf_op jit(solution)/shard_map/all_gather | solution.py:44
  160.7 2.6 %copy-start.1 = (bf16[64,16384]{1,0:T(8,128)(2,1)S(1)}, bf16[64,16384]{1,0:T(8,128)(2,1)}, u32[]{:S(2)}) copy-start(bf16[64,16384]{1,0:T(8,128)(2,1)} %all-gather.2.cloned.1.call-done) | copy-start | bytes 6291460
Sparse Core Ops, SparseCore 0:
  119.6 23.8 all-gather.1
where the time goes:
time: 208 us
  blocking collectives  64.2 us (31%)
  waiting for transfers between devices  50.6 us (24%)
  matrix products  50 us (24%)
  between operations  14.2 us (7%)
  starting transfers between devices  11.9 us (6%)
  local copies, waits for them, and re-layouts  11.7 us (6%)
  other arithmetic  4.96 us (2%)
    all_to_all x2, waiting for transfers between devices, apply_operator(): lax.all_to_all(outgoing, 'rows', split_axis=1, concat_axis=1, tiled=True)  50.1 us
    dot_general x3, matrix products, tile_products(): jnp.einsum('ktc,trc->ktr', chosen, tile_block, preferred_element_type=jnp...  36.1 us
    psum x1, blocking collectives, body(): gram_total, proj_total = lax.psum((gram_piece, proj_piece), 'rows')  35 us
    all_to_all x1, blocking collectives, apply_operator(): lax.all_to_all(outgoing, 'rows', split_axis=1, concat_axis=1, tiled=True)  29.3 us
    all_to_all x2, starting transfers between devices, apply_operator(): lax.all_to_all(outgoing, 'rows', split_axis=1, concat_axis=1, tiled=True)  11.6 us
    dot_general x3, matrix products, tile_products(): jnp.einsum('bt,ktr->kbr', onehot, products, precision=lax.Precision.HIGHEST)  9.49 us
    gather x3, local copies, waits for them, and re-layouts, tile_products(): chosen = jnp.take(sources, src_ids, axis=1)  6.1 us
  transfers between devices with their start and end apart: 3, of which 2 were waited for; matrix products, arithmetic and copies ran while one was open for 9% of the time, Pallas kernels for 0%

commit v1 on v0

--- a/solution.py
+++ b/solution.py
@@ -2,6 +2,18 @@
 import jax.numpy as jnp
 from jax import lax
 from jax.sharding import PartitionSpec as P
+
+
+def cut_along(x, dim, size):
+    dims = x.shape
+    blocks = x.reshape(*dims[:dim], size, dims[dim] // size, *dims[dim + 1 :])
+    return jnp.moveaxis(blocks, dim, 0)
+
+
+def in_order(pieces, dim):
+    pieces = jnp.moveaxis(pieces, 0, dim)
+    dims = pieces.shape
+    return pieces.reshape(*dims[:dim], dims[dim] * dims[dim + 1], *dims[dim + 2 :])
 
 
 def tile_products(sources, tile_block, row_ids, src_ids, nblocks):
@@ -18,7 +30,14 @@
     nblocks = length // tile_side
     blocked = vectors.reshape(columns, nblocks, tile_side)
     outgoing = jnp.take(blocked, send_list.reshape(-1), axis=1)
-    incoming = lax.all_to_all(outgoing, "rows", split_axis=1, concat_axis=1, tiled=True)
+    size, here = (lax.axis_size("rows"), lax.axis_index("rows"))
+    parts = cut_along(outgoing, 1, size)
+    finished = [parts[here]]
+    for step in range(1, size):
+        sent = parts[here ^ step]
+        finished.append(lax.ppermute(sent, "rows", [(i, i ^ step) for i in range(size)]))
+    parts = jnp.stack(finished)[here ^ jnp.arange(size)]
+    incoming = in_order(parts, 1)
     row_ids = tile_row.reshape(-1)
     src_ids = tile_src.reshape(-1)
     sources = jnp.concatenate([blocked, incoming], axis=1)

time: 208 us -> 206 us (level)
  starting transfers between devices: 11.9 us -> 43.5 us
  blocking collectives: 64.2 us -> 36.9 us
  waiting for transfers between devices: 50.6 us -> 38.7 us
  local copies, waits for them, and re-layouts: 11.7 us -> 18.1 us
    all_to_all x2 -> x0, waiting for transfers between devices: 50.1 us -> none  [apply_operator(): lax.all_to_all(outgoing, 'rows', split_axis=1, concat_axis=1, tiled=True)]
    ppermute x0 -> x21, starting transfers between devices: none -> 43.5 us  [apply_operator(): lax.ppermute(sent, 'rows', [(i, i ^ step) for i in range(size)])]
    ppermute x0 -> x21, waiting for transfers between devices: none -> 38.6 us  [apply_operator(): lax.ppermute(sent, 'rows', [(i, i ^ step) for i in range(size)])]
    all_to_all x1 -> x0, blocking collectives: 29.3 us -> none  [apply_operator(): lax.all_to_all(outgoing, 'rows', split_axis=1, concat_axis=1, tiled=True)]
    all_to_all x2 -> x0, starting transfers between devices: 11.6 us -> none  [apply_operator(): lax.all_to_all(outgoing, 'rows', split_axis=1, concat_axis=1, tiled=True)]
  transfers between devices with their start and end apart: 3 -> 22, of which waited for: 2 -> 7; matrix products, arithmetic and copies ran while one was open for 9% -> 11% of each run, Pallas kernels for 0% -> 0%
where the time goes in v1:
time: 206 us
  matrix products  50.4 us (24%)
  starting transfers between devices  43.5 us (21%)
  waiting for transfers between devices  38.7 us (19%)
  blocking collectives  36.9 us (18%)
  local copies, waits for them, and re-layouts  18.1 us (9%)
  between operations  14.7 us (7%)
  other arithmetic  3.84 us (2%)
    ppermute x21, starting transfers between devices, apply_operator(): lax.ppermute(sent, 'rows', [(i, i ^ step) for i in range(size)])  43.5 us
    ppermute x21, waiting for transfers between devices, apply_operator(): lax.ppermute(sent, 'rows', [(i, i ^ step) for i in range(size)])  38.6 us
    psum x1, blocking collectives, body(): gram_total, proj_total = lax.psum((gram_piece, proj_piece), 'rows')  36.9 us
    dot_general x3, matrix products, tile_products(): jnp.einsum('ktc,trc->ktr', chosen, tile_block, preferred_element_type=jnp...  36.5 us
    dot_general x3, matrix products, tile_products(): jnp.einsum('bt,ktr->kbr', onehot, products, precision=lax.Precision.HIGHEST)  9.46 us
    gather x3, local copies, waits for them, and re-layouts, tile_products(): chosen = jnp.take(sources, src_ids, axis=1)  6.14 us
  transfers between devices with their start and end apart: 22, of which 7 were waited for; matrix products, arithmetic and copies ran while one was open for 11% of the time, Pallas kernels for 0%

profile of v1, /device:TPU:0, one launch (start us, length us, event | category | flops | bytes accessed | tf_op | source)
XLA Modules:
  0.0 206.1 jit_solution(7198128277832804915)
XLA Ops:
  10.9 3.0 %collective-permute-start = (bf16[16,16,256]{2,1,0:T(8,128)(2,1)S(1)}, bf16[16,16,256]{2,1,0:T(8,128)(2,1)S(1)}, u32[]{:S(2)}, u32[]{:S(2)}) collective-permute-start(bf16[16,16,256]{2,1,0:T(8,128)(2,1)S(1)} %bitcast.212), channel_id=1, source_target_pairs={{0,4},{4,0},{8,12},{12,8},{16,20},{20,16},{24,28},{28,24},{1,5},{5... | collective-permute-start | bytes 393224 | tf_op jit(solution)/shard_map/ppermute | solution.py:38
  15.8 3.1 %collective-permute-start.3 = (bf16[16,16,256]{2,1,0:T(8,128)(2,1)S(1)}, bf16[16,16,256]{2,1,0:T(8,128)(2,1)S(1)}, u32[]{:S(2)}, u32[]{:S(2)}) collective-permute-start(bf16[16,16,256]{2,1,0:T(8,128)(2,1)S(1)} %bitcast.200), channel_id=1, source_target_pairs={{0,16},{4,20},{8,24},{12,28},{16,0},{20,4},{24,8},{28,12},{1,17},{... | collective-permute-start | bytes 393224 | tf_op jit(solution)/shard_map/ppermute | solution.py:38
  20.4 3.7 %collective-permute-start.5 = (bf16[16,16,256]{2,1,0:T(8,128)(2,1)S(1)}, bf16[16,16,256]{2,1,0:T(8,128)(2,1)S(1)}, u32[]{:S(2)}, u32[]{:S(2)}) collective-permute-start(bf16[16,16,256]{2,1,0:T(8,128)(2,1)S(1)} %bitcast.202), channel_id=1, source_target_pairs={{0,24},{4,28},{8,16},{12,20},{16,8},{20,12},{24,0},{28,4},{1,25},{... | collective-permute-start | bytes 393224 | tf_op jit(solution)/shard_map/ppermute | solution.py:38
  25.2 12.9 %collective-permute-done.4 = bf16[16,16,256]{2,1,0:T(8,128)(2,1)S(1)} collective-permute-done((bf16[16,16,256]{2,1,0:T(8,128)(2,1)S(1)}, bf16[16,16,256]{2,1,0:T(8,128)(2,1)S(1)}, u32[]{:S(2)}, u32[]{:S(2)}) %collective-permute-start.4) | collective-permute-done | bytes 131104 | tf_op jit(solution)/shard_map/ppermute | solution.py:38
  41.7 12.0 %convolution_bitcast_fusion.2 = f32[16,192,256]{2,0,1:T(8,128)S(1)} fusion(bf16[192,256,256]{2,1,0:T(8,128)(2,1)} %param.11, bf16[192,16,256]{2,1,0:T(8,128)(2,1)} %gather_fusion.4, pred[192]{0:T(512)(128)(4,1)S(1)} %compare_and_fusion), kind=kOutput, calls=%fused_computation.19 | convolution fusion | flops 403439616 | bytes 29884608 | tf_op jit(solution)/shard_map/ktc,trc->ktr/dot_general | solution.py:21
  53.8 3.1 %fusion.25 = bf16[16,64,256]{2,1,0:T(8,128)(2,1)S(1)} fusion(f32[16,192,256]{2,0,1:T(8,128)S(1)} %convolution_bitcast_fusion.2, s32[192]{0:T(256)S(1)} %bitcast.217), kind=kOutput, calls=%fused_computation.35 | convolution fusion | flops 604254208 | bytes 3670784 | tf_op jit(solution)/shard_map/bt,ktr->kbr/dot_general | solution.py:23
  59.1 4.9 %collective-permute-start.8 = (bf16[16,16,256]{2,1,0:T(8,128)(2,1)S(1)}, bf16[16,16,256]{2,1,0:T(8,128)(2,1)S(1)}, u32[]{:S(2)}, u32[]{:S(2)}) collective-permute-start(bf16[16,16,256]{2,1,0:T(8,128)(2,1)S(1)} %bitcast.213), channel_id=1, source_target_pairs={{0,8},{4,12},{8,0},{12,4},{16,24},{20,28},{24,16},{28,20},{1,9},{5... | collective-permute-start | bytes 393224 | tf_op jit(solution)/shard_map/ppermute | solution.py:38
  65.2 3.6 %collective-permute-start.10 = (bf16[16,16,256]{2,1,0:T(8,128)(2,1)S(1)}, bf16[16,16,256]{2,1,0:T(8,128)(2,1)S(1)}, u32[]{:S(2)}, u32[]{:S(2)}) collective-permute-start(bf16[16,16,256]{2,1,0:T(8,128)(2,1)S(1)} %bitcast.207), channel_id=1, source_target_pairs={{0,16},{4,20},{8,24},{12,28},{16,0},{20,4},{24,8},{28,12},{1,17},{... | collective-permute-start | bytes 393224 | tf_op jit(solution)/shard_map/ppermute | solution.py:38
  69.1 2.4 %collective-permute-start.12 = (bf16[16,16,256]{2,1,0:T(8,128)(2,1)S(1)}, bf16[16,16,256]{2,1,0:T(8,128)(2,1)S(1)}, u32[]{:S(2)}, u32[]{:S(2)}) collective-permute-start(bf16[16,16,256]{2,1,0:T(8,128)(2,1)S(1)} %bitcast.203), channel_id=1, source_target_pairs={{0,24},{4,28},{8,16},{12,20},{16,8},{20,12},{24,0},{28,4},{1,25},{... | collective-permute-start | bytes 393224 | tf_op jit(solution)/shard_map/ppermute | solution.py:38
  71.5 2.5 %collective-permute-start.13 = (bf16[16,16,256]{2,1,0:T(8,128)(2,1)S(1)}, bf16[16,16,256]{2,1,0:T(8,128)(2,1)S(1)}, u32[]{:S(2)}, u32[]{:S(2)}) collective-permute-start(bf16[16,16,256]{2,1,0:T(8,128)(2,1)S(1)} %bitcast.196), channel_id=1, source_target_pairs={{0,28},{4,24},{8,20},{12,16},{16,12},{20,8},{24,4},{28,0},{1,29},{... | collective-permute-start | bytes 393224 | tf_op jit(solution)/shard_map/ppermute | solution.py:38
  74.1 9.6 %collective-permute-done.10 = bf16[16,16,256]{2,1,0:T(8,128)(2,1)S(1)} collective-permute-done((bf16[16,16,256]{2,1,0:T(8,128)(2,1)S(1)}, bf16[16,16,256]{2,1,0:T(8,128)(2,1)S(1)}, u32[]{:S(2)}, u32[]{:S(2)}) %collective-permute-start.10) | collective-permute-done | bytes 131104 | tf_op jit(solution)/shard_map/ppermute | solution.py:38
  83.8 3.0 %collective-permute-done.11 = bf16[16,16,256]{2,1,0:T(8,128)(2,1)S(1)} collective-permute-done((bf16[16,16,256]{2,1,0:T(8,128)(2,1)S(1)}, bf16[16,16,256]{2,1,0:T(8,128)(2,1)S(1)}, u32[]{:S(2)}, u32[]{:S(2)}) %collective-permute-start.11) | collective-permute-done | bytes 131104 | tf_op jit(solution)/shard_map/ppermute | solution.py:38
  90.4 12.2 %convolution_bitcast_fusion.1 = f32[16,192,256]{2,0,1:T(8,128)S(1)} fusion(bf16[192,256,256]{2,1,0:T(8,128)(2,1)} %param.11, bf16[192,16,256]{2,1,0:T(8,128)(2,1)} %gather_fusion.6, pred[192]{0:T(512)(128)(4,1)S(1)} %compare_and_fusion), kind=kOutput, calls=%fused_computation.18 | convolution fusion | flops 403439616 | bytes 29884608 | tf_op jit(solution)/shard_map/ktc,trc->ktr/dot_general | solution.py:21
  102.6 3.2 %fusion.16 = f32[16,256,64]{1,2,0:T(8,128)S(1)} fusion(f32[16,192,256]{2,0,1:T(8,128)S(1)} %convolution_bitcast_fusion.1, s32[192]{0:T(256)S(1)} %bitcast.218), kind=kOutput, calls=%fused_computation.32 | convolution fusion | flops 604254208 | bytes 4195072 | tf_op jit(solution)/shard_map/bt,ktr->kbr/dot_general | solution.py:23
  111.2 4.6 %collective-permute-start.15 = (bf16[16,16,256]{2,1,0:T(8,128)(2,1)S(1)}, bf16[16,16,256]{2,1,0:T(8,128)(2,1)S(1)}, u32[]{:S(2)}, u32[]{:S(2)}) collective-permute-start(bf16[16,16,256]{2,1,0:T(8,128)(2,1)S(1)} %bitcast.214), channel_id=1, source_target_pairs={{0,8},{4,12},{8,0},{12,4},{16,24},{20,28},{24,16},{28,20},{1,9},{5... | collective-permute-start | bytes 393224 | tf_op jit(solution)/shard_map/ppermute | solution.py:38
  116.8 2.2 %collective-permute-start.17 = (bf16[16,16,256]{2,1,0:T(8,128)(2,1)S(1)}, bf16[16,16,256]{2,1,0:T(8,128)(2,1)S(1)}, u32[]{:S(2)}, u32[]{:S(2)}) collective-permute-start(bf16[16,16,256]{2,1,0:T(8,128)(2,1)S(1)} %bitcast.208), channel_id=1, source_target_pairs={{0,16},{4,20},{8,24},{12,28},{16,0},{20,4},{24,8},{28,12},{1,17},{... | collective-permute-start | bytes 393224 | tf_op jit(solution)/shard_map/ppermute | solution.py:38
  120.1 2.1 %collective-permute-start.19 = (bf16[16,16,256]{2,1,0:T(8,128)(2,1)S(1)}, bf16[16,16,256]{2,1,0:T(8,128)(2,1)S(1)}, u32[]{:S(2)}, u32[]{:S(2)}) collective-permute-start(bf16[16,16,256]{2,1,0:T(8,128)(2,1)S(1)} %bitcast.204), channel_id=1, source_target_pairs={{0,24},{4,28},{8,16},{12,20},{16,8},{20,12},{24,0},{28,4},{1,25},{... | collective-permute-start | bytes 393224 | tf_op jit(solution)/shard_map/ppermute | solution.py:38
  122.2 2.7 %collective-permute-start.20 = (bf16[16,16,256]{2,1,0:T(8,128)(2,1)S(1)}, bf16[16,16,256]{2,1,0:T(8,128)(2,1)S(1)}, u32[]{:S(2)}, u32[]{:S(2)}) collective-permute-start(bf16[16,16,256]{2,1,0:T(8,128)(2,1)S(1)} %bitcast.197), channel_id=1, source_target_pairs={{0,28},{4,24},{8,20},{12,16},{16,12},{20,8},{24,4},{28,0},{1,29},{... | collective-permute-start | bytes 393224 | tf_op jit(solution)/shard_map/ppermute | solution.py:38
  125.8 9.0 %collective-permute-done.17 = bf16[16,16,256]{2,1,0:T(8,128)(2,1)S(1)} collective-permute-done((bf16[16,16,256]{2,1,0:T(8,128)(2,1)S(1)}, bf16[16,16,256]{2,1,0:T(8,128)(2,1)S(1)}, u32[]{:S(2)}, u32[]{:S(2)}) %collective-permute-start.17) | collective-permute-done | bytes 131104 | tf_op jit(solution)/shard_map/ppermute | solution.py:38
  134.7 2.7 %collective-permute-done.18 = bf16[16,16,256]{2,1,0:T(8,128)(2,1)S(1)} collective-permute-done((bf16[16,16,256]{2,1,0:T(8,128)(2,1)S(1)}, bf16[16,16,256]{2,1,0:T(8,128)(2,1)S(1)}, u32[]{:S(2)}, u32[]{:S(2)}) %collective-permute-start.18) | collective-permute-done | bytes 131104 | tf_op jit(solution)/shard_map/ppermute | solution.py:38
  141.0 12.3 %convolution_bitcast_fusion = f32[16,192,256]{2,0,1:T(8,128)S(1)} fusion(bf16[192,256,256]{2,1,0:T(8,128)(2,1)} %param.11, bf16[192,16,256]{2,1,0:T(8,128)(2,1)} %gather_fusion.8, pred[192]{0:T(512)(128)(4,1)S(1)} %compare_and_fusion), kind=kOutput, calls=%fused_computation.17 | convolution fusion | flops 403439616 | bytes 29884608 | tf_op jit(solution)/shard_map/ktc,trc->ktr/dot_general | solution.py:21
  153.2 3.2 %fusion.22 = bf16[16,256,64]{1,2,0:T(8,128)(2,1)S(1)} fusion(f32[16,192,256]{2,0,1:T(8,128)S(1)} %convolution_bitcast_fusion, s32[192]{0:T(256)S(1)} %bitcast.219), kind=kOutput, calls=%fused_computation.34 | convolution fusion | flops 604254208 | bytes 3670784 | tf_op jit(solution)/shard_map/bt,ktr->kbr/dot_general | solution.py:23
  156.7 2.5 %fusion.42 = f32[16,64]{1,0:T(8,128)S(1)} fusion(bf16[16,16384]{1,0:T(8,128)(2,1)} %subtract_convert_fusion, bf16[64,16384]{1,0:T(8,128)(2,1)} %all-gather.2.cloned.1.call-done), kind=kOutput, calls=%fused_computation.133 | convolution fusion | flops 33554432 | bytes 2625536 | tf_op jit(solution)/shard_map/dot_general | solution.py:48
  159.9 36.9 %all-reduce = (f32[16,64]{1,0:T(8,128)S(1)}, f32[16,64]{1,0:T(8,128)S(1)}) all-reduce(f32[16,64]{1,0:T(8,128)S(1)} %fusion.42, f32[16,64]{1,0:T(8,128)S(1)} %fusion.43), channel_id=1, replica_groups=mesh['rows'=8,'cols'=4] {'rows'}, use_global_device_ids=true, to_apply=%region_0.3 | all-reduce | flops 2048 | bytes 16384 | tf_op jit(solution)/shard_map/psum | solution.py:69
  (126 shorter events, 34.0 us)
Async XLA Ops:
  7.2 190.9 %copy-start = (bf16[64,16]{0,1:T(8,128)(2,1)S(1)}, bf16[64,16]{0,1:T(8,128)(2,1)}, u32[]{:S(2)}) copy-start(bf16[64,16]{0,1:T(8,128)(2,1)} %param.15) | copy-start | bytes 6148
  7.2 149.5 %all-gather.2.cloned.1.call-start = ((), (), s32[]{:S(2)}) async-start(), calls=%async_computation | async-start | bytes 2621440 | tf_op jit(solution)/shard_map/all_gather | solution.py:63
  10.9 9.5 %collective-permute-start = (bf16[16,16,256]{2,1,0:T(8,128)(2,1)S(1)}, bf16[16,16,256]{2,1,0:T(8,128)(2,1)S(1)}, u32[]{:S(2)}, u32[]{:S(2)}) collective-permute-start(bf16[16,16,256]{2,1,0:T(8,128)(2,1)S(1)} %bitcast.212), channel_id=1, source_target_pairs={{0,4},{4,0},{8,12},{12,8},{16,20},{20,16},{24,28},{28,24},{1,5},{5... | collective-permute-start | bytes 393224 | tf_op jit(solution)/shard_map/ppermute | solution.py:38
  14.0 10.7 %collective-permute-start.1 = (bf16[16,16,256]{2,1,0:T(8,128)(2,1)S(1)}, bf16[16,16,256]{2,1,0:T(8,128)(2,1)S(1)}, u32[]{:S(2)}, u32[]{:S(2)}) collective-permute-start(bf16[16,16,256]{2,1,0:T(8,128)(2,1)S(1)} %bitcast.209), channel_id=1, source_target_pairs={{0,8},{4,12},{8,0},{12,4},{16,24},{20,28},{24,16},{28,20},{1,9},{5... | collective-permute-start | bytes 393224 | tf_op jit(solution)/shard_map/ppermute | solution.py:38
  15.6 9.5 %collective-permute-start.2 = (bf16[16,16,256]{2,1,0:T(8,128)(2,1)S(1)}, bf16[16,16,256]{2,1,0:T(8,128)(2,1)S(1)}, u32[]{:S(2)}, u32[]{:S(2)}) collective-permute-start(bf16[16,16,256]{2,1,0:T(8,128)(2,1)S(1)} %bitcast.201), channel_id=1, source_target_pairs={{0,12},{4,8},{8,4},{12,0},{16,28},{20,24},{24,20},{28,16},{1,13},{... | collective-permute-start | bytes 393224 | tf_op jit(solution)/shard_map/ppermute | solution.py:38
  15.8 9.4 %collective-permute-start.3 = (bf16[16,16,256]{2,1,0:T(8,128)(2,1)S(1)}, bf16[16,16,256]{2,1,0:T(8,128)(2,1)S(1)}, u32[]{:S(2)}, u32[]{:S(2)}) collective-permute-start(bf16[16,16,256]{2,1,0:T(8,128)(2,1)S(1)} %bitcast.200), channel_id=1, source_target_pairs={{0,16},{4,20},{8,24},{12,28},{16,0},{20,4},{24,8},{28,12},{1,17},{... | collective-permute-start | bytes 393224 | tf_op jit(solution)/shard_map/ppermute | solution.py:38
  18.9 19.2 %collective-permute-start.4 = (bf16[16,16,256]{2,1,0:T(8,128)(2,1)S(1)}, bf16[16,16,256]{2,1,0:T(8,128)(2,1)S(1)}, u32[]{:S(2)}, u32[]{:S(2)}) collective-permute-start(bf16[16,16,256]{2,1,0:T(8,128)(2,1)S(1)} %bitcast.198), channel_id=1, source_target_pairs={{0,20},{4,16},{8,28},{12,24},{16,4},{20,0},{24,12},{28,8},{1,21},{... | collective-permute-start | bytes 393224 | tf_op jit(solution)/shard_map/ppermute | solution.py:38
  20.4 17.7 %collective-permute-start.5 = (bf16[16,16,256]{2,1,0:T(8,128)(2,1)S(1)}, bf16[16,16,256]{2,1,0:T(8,128)(2,1)S(1)}, u32[]{:S(2)}, u32[]{:S(2)}) collective-permute-start(bf16[16,16,256]{2,1,0:T(8,128)(2,1)S(1)} %bitcast.202), channel_id=1, source_target_pairs={{0,24},{4,28},{8,16},{12,20},{16,8},{20,12},{24,0},{28,4},{1,25},{... | collective-permute-start | bytes 393224 | tf_op jit(solution)/shard_map/ppermute | solution.py:38
  24.6 13.5 %collective-permute-start.6 = (bf16[16,16,256]{2,1,0:T(8,128)(2,1)S(1)}, bf16[16,16,256]{2,1,0:T(8,128)(2,1)S(1)}, u32[]{:S(2)}, u32[]{:S(2)}) collective-permute-start(bf16[16,16,256]{2,1,0:T(8,128)(2,1)S(1)} %bitcast.199), channel_id=1, source_target_pairs={{0,28},{4,24},{8,20},{12,16},{16,12},{20,8},{24,4},{28,0},{1,29},{... | collective-permute-start | bytes 393224 | tf_op jit(solution)/shard_map/ppermute | solution.py:38
  41.7 12.1 %copy-start.3 = (s32[1,192]{1,0:T(1,128)S(1)}, s32[1,192]{1,0:T(1,128)}, u32[]{:S(2)}) copy-start(s32[1,192]{1,0:T(1,128)} %param.12) | copy-start | bytes 2308
  58.2 10.9 %collective-permute-start.7 = (bf16[16,16,256]{2,1,0:T(8,128)(2,1)S(1)}, bf16[16,16,256]{2,1,0:T(8,128)(2,1)S(1)}, u32[]{:S(2)}, u32[]{:S(2)}) collective-permute-start(bf16[16,16,256]{2,1,0:T(8,128)(2,1)S(1)} %bitcast.215), channel_id=1, source_target_pairs={{0,4},{4,0},{8,12},{12,8},{16,20},{20,16},{24,28},{28,24},{1,5},{5... | collective-permute-start | bytes 393224 | tf_op jit(solution)/shard_map/ppermute | solution.py:38
  59.1 12.4 %collective-permute-start.8 = (bf16[16,16,256]{2,1,0:T(8,128)(2,1)S(1)}, bf16[16,16,256]{2,1,0:T(8,128)(2,1)S(1)}, u32[]{:S(2)}, u32[]{:S(2)}) collective-permute-start(bf16[16,16,256]{2,1,0:T(8,128)(2,1)S(1)} %bitcast.213), channel_id=1, source_target_pairs={{0,8},{4,12},{8,0},{12,4},{16,24},{20,28},{24,16},{28,20},{1,9},{5... | collective-permute-start | bytes 393224 | tf_op jit(solution)/shard_map/ppermute | solution.py:38
  64.1 10.0 %collective-permute-start.9 = (bf16[16,16,256]{2,1,0:T(8,128)(2,1)S(1)}, bf16[16,16,256]{2,1,0:T(8,128)(2,1)S(1)}, u32[]{:S(2)}, u32[]{:S(2)}) collective-permute-start(bf16[16,16,256]{2,1,0:T(8,128)(2,1)S(1)} %bitcast.210), channel_id=1, source_target_pairs={{0,12},{4,8},{8,4},{12,0},{16,28},{20,24},{24,20},{28,16},{1,13},{... | collective-permute-start | bytes 393224 | tf_op jit(solution)/shard_map/ppermute | solution.py:38
  65.2 18.6 %collective-permute-start.10 = (bf16[16,16,256]{2,1,0:T(8,128)(2,1)S(1)}, bf16[16,16,256]{2,1,0:T(8,128)(2,1)S(1)}, u32[]{:S(2)}, u32[]{:S(2)}) collective-permute-start(bf16[16,16,256]{2,1,0:T(8,128)(2,1)S(1)} %bitcast.207), channel_id=1, source_target_pairs={{0,16},{4,20},{8,24},{12,28},{16,0},{20,4},{24,8},{28,12},{1,17},{... | collective-permute-start | bytes 393224 | tf_op jit(solution)/shard_map/ppermute | solution.py:38
  68.8 17.9 %collective-permute-start.11 = (bf16[16,16,256]{2,1,0:T(8,128)(2,1)S(1)}, bf16[16,16,256]{2,1,0:T(8,128)(2,1)S(1)}, u32[]{:S(2)}, u32[]{:S(2)}) collective-permute-start(bf16[16,16,256]{2,1,0:T(8,128)(2,1)S(1)} %bitcast.205), channel_id=1, source_target_pairs={{0,20},{4,16},{8,28},{12,24},{16,4},{20,0},{24,12},{28,8},{1,21},{... | collective-permute-start | bytes 393224 | tf_op jit(solution)/shard_map/ppermute | solution.py:38
  69.1 17.7 %collective-permute-start.12 = (bf16[16,16,256]{2,1,0:T(8,128)(2,1)S(1)}, bf16[16,16,256]{2,1,0:T(8,128)(2,1)S(1)}, u32[]{:S(2)}, u32[]{:S(2)}) collective-permute-start(bf16[16,16,256]{2,1,0:T(8,128)(2,1)S(1)} %bitcast.203), channel_id=1, source_target_pairs={{0,24},{4,28},{8,16},{12,20},{16,8},{20,12},{24,0},{28,4},{1,25},{... | collective-permute-start | bytes 393224 | tf_op jit(solution)/shard_map/ppermute | solution.py:38
  71.5 15.3 %collective-permute-start.13 = (bf16[16,16,256]{2,1,0:T(8,128)(2,1)S(1)}, bf16[16,16,256]{2,1,0:T(8,128)(2,1)S(1)}, u32[]{:S(2)}, u32[]{:S(2)}) collective-permute-start(bf16[16,16,256]{2,1,0:T(8,128)(2,1)S(1)} %bitcast.196), channel_id=1, source_target_pairs={{0,28},{4,24},{8,20},{12,16},{16,12},{20,8},{24,4},{28,0},{1,29},{... | collective-permute-start | bytes 393224 | tf_op jit(solution)/shard_map/ppermute | solution.py:38
  109.8 10.2 %collective-permute-start.14 = (bf16[16,16,256]{2,1,0:T(8,128)(2,1)S(1)}, bf16[16,16,256]{2,1,0:T(8,128)(2,1)S(1)}, u32[]{:S(2)}, u32[]{:S(2)}) collective-permute-start(bf16[16,16,256]{2,1,0:T(8,128)(2,1)S(1)} %bitcast.216), channel_id=1, source_target_pairs={{0,4},{4,0},{8,12},{12,8},{16,20},{20,16},{24,28},{28,24},{1,5},{5... | collective-permute-start | bytes 393224 | tf_op jit(solution)/shard_map/ppermute | solution.py:38
  111.2 11.0 %collective-permute-start.15 = (bf16[16,16,256]{2,1,0:T(8,128)(2,1)S(1)}, bf16[16,16,256]{2,1,0:T(8,128)(2,1)S(1)}, u32[]{:S(2)}, u32[]{:S(2)}) collective-permute-start(bf16[16,16,256]{2,1,0:T(8,128)(2,1)S(1)} %bitcast.214), channel_id=1, source_target_pairs={{0,8},{4,12},{8,0},{12,4},{16,24},{20,28},{24,16},{28,20},{1,9},{5... | collective-permute-start | bytes 393224 | tf_op jit(solution)/shard_map/ppermute | solution.py:38
  115.8 10.0 %collective-permute-start.16 = (bf16[16,16,256]{2,1,0:T(8,128)(2,1)S(1)}, bf16[16,16,256]{2,1,0:T(8,128)(2,1)S(1)}, u32[]{:S(2)}, u32[]{:S(2)}) collective-permute-start(bf16[16,16,256]{2,1,0:T(8,128)(2,1)S(1)} %bitcast.211), channel_id=1, source_target_pairs={{0,12},{4,8},{8,4},{12,0},{16,28},{20,24},{24,20},{28,16},{1,13},{... | collective-permute-start | bytes 393224 | tf_op jit(solution)/shard_map/ppermute | solution.py:38
  116.8 18.0 %collective-permute-start.17 = (bf16[16,16,256]{2,1,0:T(8,128)(2,1)S(1)}, bf16[16,16,256]{2,1,0:T(8,128)(2,1)S(1)}, u32[]{:S(2)}, u32[]{:S(2)}) collective-permute-start(bf16[16,16,256]{2,1,0:T(8,128)(2,1)S(1)} %bitcast.208), channel_id=1, source_target_pairs={{0,16},{4,20},{8,24},{12,28},{16,0},{20,4},{24,8},{28,12},{1,17},{... | collective-permute-start | bytes 393224 | tf_op jit(solution)/shard_map/ppermute | solution.py:38
  119.0 18.4 %collective-permute-start.18 = (bf16[16,16,256]{2,1,0:T(8,128)(2,1)S(1)}, bf16[16,16,256]{2,1,0:T(8,128)(2,1)S(1)}, u32[]{:S(2)}, u32[]{:S(2)}) collective-permute-start(bf16[16,16,256]{2,1,0:T(8,128)(2,1)S(1)} %bitcast.206), channel_id=1, source_target_pairs={{0,20},{4,16},{8,28},{12,24},{16,4},{20,0},{24,12},{28,8},{1,21},{... | collective-permute-start | bytes 393224 | tf_op jit(solution)/shard_map/ppermute | solution.py:38
  120.1 17.4 %collective-permute-start.19 = (bf16[16,16,256]{2,1,0:T(8,128)(2,1)S(1)}, bf16[16,16,256]{2,1,0:T(8,128)(2,1)S(1)}, u32[]{:S(2)}, u32[]{:S(2)}) collective-permute-start(bf16[16,16,256]{2,1,0:T(8,128)(2,1)S(1)} %bitcast.204), channel_id=1, source_target_pairs={{0,24},{4,28},{8,16},{12,20},{16,8},{20,12},{24,0},{28,4},{1,25},{... | collective-permute-start | bytes 393224 | tf_op jit(solution)/shard_map/ppermute | solution.py:38
  122.2 15.3 %collective-permute-start.20 = (bf16[16,16,256]{2,1,0:T(8,128)(2,1)S(1)}, bf16[16,16,256]{2,1,0:T(8,128)(2,1)S(1)}, u32[]{:S(2)}, u32[]{:S(2)}) collective-permute-start(bf16[16,16,256]{2,1,0:T(8,128)(2,1)S(1)} %bitcast.197), channel_id=1, source_target_pairs={{0,28},{4,24},{8,20},{12,16},{16,12},{20,8},{24,4},{28,0},{1,29},{... | collective-permute-start | bytes 393224 | tf_op jit(solution)/shard_map/ppermute | solution.py:38
  (3 other events, 13.1 us)
Sparse Core Ops, SparseCore 0:
  107.8 25.0 all-gather.1
